TPU v7x, 128 devices: a whole 4x4x4 slice. The times are simulated.
128 devices in a mesh: ctx: 32 (over z, y_hi, x), ch: 4 (over y_lo, core).
Axes of the slice: x: 4, y: 4 (y_hi: 2, y_lo: 2; y = y_hi * 2 + y_lo), z: 4, core: 2. Of those that a mesh axis runs over, the one named last changes fastest.
Arguments:
- q_conv: bfloat16 [7168, 4096], P('ctx', 'ch'), may hold values from -6 to 6
- k_conv: bfloat16 [7168, 4096], P('ctx', 'ch'), may hold values from -6 to 6
- v_conv: bfloat16 [7168, 4096], P('ctx', 'ch'), may hold values from -6 to 6
- conv_filter: bfloat16 [7168, 256], P('ctx', 'ch'), may hold values from -1 to 1
- q_attn: bfloat16 [7168, 4096], P('ctx', 'ch'), may hold values from -5 to 5
- k_attn: bfloat16 [7168, 4096], P('ctx', 'ch'), may hold values from -5 to 5
- v_attn: bfloat16 [7168, 4096], P('ctx', 'ch'), may hold values from -6 to 6
- w_conv_out: bfloat16 [4096, 4096], P('ch'), may hold values from -0.09375 to 0.09375
- w_attn_out: bfloat16 [4096, 4096], P('ch'), may hold values from -0.375 to 0.375
Outputs:
- layer_out: bfloat16 [7168, 4096], P(('ctx', 'ch'))
All inputs are finite; a program needn't handle non-finite values.
Results may differ from a plain program's by a relative error of at most 0.018.
Values may be sent and summed in bfloat16 or wider, within the bound.
No kernel may reach another device: no remote copies, remote signals or barrier semaphores. Data moves between devices by JAX's collectives and lax.ppermute only.
A program may use at most 192 MiB of HBM per device.

v0:
```python
from functools import partial
import math
import jax
import jax.numpy as jnp
from jax import lax
from jax.sharding import PartitionSpec as P

HD = 128
two_pi = 2.0 * math.pi
neg_large = -1e30
highest = lax.Precision.HIGHEST


def angle_table(left_idx, right_idx, period):
    product = left_idx[:, None] * right_idx[None, :] % period
    return product.astype(jnp.float32) * (two_pi / period)


def section_coarse(values, cos_table, sin_table, twiddle):
    real_part = jnp.einsum("kn,nsc->ksc", cos_table, values, precision=highest)
    imag_part = -jnp.einsum("kn,nsc->ksc", sin_table, values, precision=highest)
    cos_twist = jnp.cos(twiddle)[:, :, None]
    sin_twist = jnp.sin(twiddle)[:, :, None]
    return (
        real_part * cos_twist + imag_part * sin_twist,
        imag_part * cos_twist - real_part * sin_twist,
    )


def section_fine(real_part, imag_part, cos_table, sin_table, direction):
    cos_real = jnp.einsum("kn,anc->akc", cos_table, real_part, precision=highest)
    cos_imag = jnp.einsum("kn,anc->akc", cos_table, imag_part, precision=highest)
    sin_real = jnp.einsum("kn,anc->akc", sin_table, real_part, precision=highest)
    sin_imag = jnp.einsum("kn,anc->akc", sin_table, imag_part, precision=highest)
    return (cos_real - direction * sin_imag, cos_imag + direction * sin_real)


def spectral_conv(gated, filters, my_index, tok_rows, count_ctx):
    chans = gated.shape[1]
    groups = filters.shape[1]
    share = chans // groups
    sub_rows = tok_rows // count_ctx
    period = 2 * count_ctx * tok_rows
    got_source, got_filter = (
        lax.all_to_all(
            gated.reshape(1, tok_rows, chans), "ctx", split_axis=1, concat_axis=0, tiled=True
        ),
        lax.all_to_all(
            filters.reshape(1, tok_rows, groups), "ctx", split_axis=1, concat_axis=0, tiled=True
        ),
    )
    coarse_idx = jnp.arange(count_ctx, dtype=jnp.int32)
    coarse_freq = jnp.arange(2 * count_ctx, dtype=jnp.int32)
    coarse_angle = angle_table(coarse_freq, coarse_idx, 2 * count_ctx)
    cos_coarse = jnp.cos(coarse_angle)
    sin_coarse = jnp.sin(coarse_angle)
    fine_global = my_index * sub_rows + jnp.arange(sub_rows, dtype=jnp.int32)
    twist_in = angle_table(coarse_freq, fine_global, period)
    source_re, source_im = section_coarse(
        got_source.astype(jnp.float32), cos_coarse, sin_coarse, twist_in
    )
    filter_re, filter_im = section_coarse(
        got_filter.astype(jnp.float32), cos_coarse, sin_coarse, twist_in
    )
    source_re, source_im, filter_re, filter_im = (
        lax.all_to_all(
            source_re.astype(jnp.bfloat16), "ctx", split_axis=0, concat_axis=1, tiled=True
        ).astype(source_re.dtype),
        lax.all_to_all(
            source_im.astype(jnp.bfloat16), "ctx", split_axis=0, concat_axis=1, tiled=True
        ).astype(source_im.dtype),
        lax.all_to_all(
            filter_re.astype(jnp.bfloat16), "ctx", split_axis=0, concat_axis=1, tiled=True
        ).astype(filter_re.dtype),
        lax.all_to_all(
            filter_im.astype(jnp.bfloat16), "ctx", split_axis=0, concat_axis=1, tiled=True
        ).astype(filter_im.dtype),
    )
    fine_idx = jnp.arange(tok_rows, dtype=jnp.int32)
    fine_angle = angle_table(fine_idx, fine_idx, tok_rows)
    cos_fine = jnp.cos(fine_angle)
    sin_fine = jnp.sin(fine_angle)
    source_re, source_im = section_fine(source_re, source_im, cos_fine, sin_fine, -1.0)
    filter_re, filter_im = section_fine(filter_re, filter_im, cos_fine, sin_fine, -1.0)
    split_re = source_re.reshape(2, tok_rows, groups, share)
    split_im = source_im.reshape(2, tok_rows, groups, share)
    prod_re = split_re * filter_re[..., None] - split_im * filter_im[..., None]
    prod_im = split_re * filter_im[..., None] + split_im * filter_re[..., None]
    back_re, back_im = section_fine(
        prod_re.reshape(2, tok_rows, chans),
        prod_im.reshape(2, tok_rows, chans),
        cos_fine,
        sin_fine,
        1.0,
    )
    pair_freq = my_index * 2 + jnp.arange(2, dtype=jnp.int32)
    twist_out = angle_table(pair_freq, fine_idx, period)
    cos_out = jnp.cos(twist_out)[:, :, None]
    sin_out = jnp.sin(twist_out)[:, :, None]
    turned_re = back_re * cos_out - back_im * sin_out
    turned_im = back_re * sin_out + back_im * cos_out
    turned_re, turned_im = (
        lax.all_to_all(
            turned_re.astype(jnp.bfloat16), "ctx", split_axis=1, concat_axis=0, tiled=True
        ).astype(turned_re.dtype),
        lax.all_to_all(
            turned_im.astype(jnp.bfloat16), "ctx", split_axis=1, concat_axis=0, tiled=True
        ).astype(turned_im.dtype),
    )
    result = jnp.einsum("nk,ksc->nsc", cos_coarse.T, turned_re, precision=highest)
    result = result - jnp.einsum("nk,ksc->nsc", sin_coarse.T, turned_im, precision=highest)
    rounded = (result / period).astype(jnp.bfloat16)
    returned = lax.all_to_all(rounded, "ctx", split_axis=0, concat_axis=1, tiled=True)
    return returned.reshape(tok_rows, chans)


def keep_same(running):
    return running


def attend_block(group_query, group_pos, key_block, value_block, key_pos, score_scale, group_state):
    run_max, run_total, run_accum = group_state
    scores = (
        jnp.einsum("thd,shd->hts", group_query, key_block, preferred_element_type=jnp.float32)
        * score_scale
    )
    allowed = (key_pos[None, :] <= group_pos[:, None])[None]
    block_max = jnp.max(jnp.where(allowed, scores, neg_large), axis=2)
    new_max = jnp.maximum(run_max, block_max)
    factor = jnp.exp(run_max - new_max)
    weights = jnp.where(allowed, jnp.exp(scores - new_max[:, :, None]), 0.0)
    new_total = run_total * factor + jnp.sum(weights, axis=2)
    new_accum = run_accum * factor[:, :, None] + jnp.einsum(
        "hts,shd->htd",
        weights.astype(jnp.bfloat16),
        value_block,
        preferred_element_type=jnp.float32,
    )
    return (new_max, new_total, new_accum)


def attention(q_attn, k_attn, v_attn, my_index, tok_rows):
    heads_local = q_attn.shape[1] // HD
    score_scale = HD ** (-0.5)
    queries = q_attn.reshape(tok_rows, heads_local, HD)
    group_list = [(queries, my_index * tok_rows + jnp.arange(tok_rows, dtype=jnp.int32))]
    initial = tuple(
        (
            (
                jnp.full((heads_local, entry[0].shape[0]), neg_large, jnp.float32),
                jnp.zeros((heads_local, entry[0].shape[0]), jnp.float32),
                jnp.zeros((heads_local, entry[0].shape[0], HD), jnp.float32),
            )
            for entry in group_list
        )
    )
    key_piece = lax.all_gather(k_attn, "ctx", axis=0, tiled=True)
    value_piece = lax.all_gather(v_attn, "ctx", axis=0, tiled=True)
    count_blocks = key_piece.shape[0] // tok_rows
    keys_split = key_piece.reshape(count_blocks, tok_rows, heads_local, HD)
    values_split = value_piece.reshape(count_blocks, tok_rows, heads_local, HD)

    def one_block(carry, item):
        key_block, value_block, block_number = item
        block_first = block_number * tok_rows
        key_pos = block_first + jnp.arange(tok_rows, dtype=jnp.int32)
        updated = []
        for entry, group_state in zip(group_list, carry):
            step_fn = partial(
                attend_block, entry[0], entry[1], key_block, value_block, key_pos, score_scale
            )
            updated.append(lax.cond(block_first <= entry[1][-1], step_fn, keep_same, group_state))
        return (tuple(updated), None)

    new_state, unused = lax.scan(
        one_block, initial, (keys_split, values_split, jnp.arange(count_blocks, dtype=jnp.int32))
    )
    outputs = [
        (state[2] / state[1][:, :, None]).transpose(1, 0, 2).astype(jnp.bfloat16)
        for state in new_state
    ]
    merged = outputs[0]
    return merged.reshape(tok_rows, heads_local * HD)


def local(q_conv, k_conv, v_conv, conv_filter, q_attn, k_attn, v_attn, w_conv_out, w_attn_out):
    count_ctx = lax.axis_size("ctx")
    my_index = lax.axis_index("ctx")
    tok_rows = q_conv.shape[0]
    gated = (k_conv.astype(jnp.float32) * v_conv.astype(jnp.float32)).astype(jnp.bfloat16)
    conv = spectral_conv(gated, conv_filter, my_index, tok_rows, count_ctx)
    mixed = (q_conv.astype(jnp.float32) * conv.astype(jnp.float32)).astype(jnp.bfloat16)
    attended = attention(q_attn, k_attn, v_attn, my_index, tok_rows)
    return lax.psum_scatter(
        (
            jnp.dot(mixed, w_conv_out, preferred_element_type=jnp.float32)
            + jnp.dot(attended, w_attn_out, preferred_element_type=jnp.float32)
        ).astype(jnp.bfloat16),
        "ch",
        scatter_dimension=0,
        tiled=True,
    )


def solution(mesh):
    return jax.shard_map(
        local,
        mesh=mesh,
        in_specs=(
            P("ctx", "ch"),
            P("ctx", "ch"),
            P("ctx", "ch"),
            P("ctx", "ch"),
            P("ctx", "ch"),
            P("ctx", "ch"),
            P("ctx", "ch"),
            P("ch", None),
            P("ch", None),
        ),
        out_specs=P(("ctx", "ch"), None),
        check_vma=False,
    )
```

profile of v0, /device:TPU:1, one launch (start us, length us, event | category | flops | bytes accessed | tf_op | source)
XLA Modules:
  0.0 611.6 jit_solution(7817200553837334792)
XLA Ops:
  11.1 11.3 %all-to-all-start.3 = ((bf16[32,2,224]{2,1,0:T(2,128)(2,1)}), bf16[32,2,224]{2,1,0:T(2,128)(2,1)S(1)}, u32[]{:S(2)}, u32[]{:S(2)}) async-start(bf16[32,2,224]{2,1,0:T(2,128)(2,1)} %reshape.188), calls=%async_computation.3 | async-start | bytes 65536 | tf_op jit(solution)/shard_map/all_to_all | solution.py:48
  24.6 3.3 reduce.5
  29.0 2.2 all-to-all-done.3
  31.3 7.0 %all-to-all-start = ((bf16[32,2,3584]{2,1,0:T(2,128)(2,1)}), bf16[32,2,3584]{2,1,0:T(2,128)(2,1)S(1)}, u32[]{:S(2)}, u32[]{:S(2)}) async-start(bf16[32,2,3584]{2,1,0:T(2,128)(2,1)} %reshape.194), calls=%async_computation | async-start | bytes 917504 | tf_op jit(solution)/shard_map/all_to_all | solution.py:45
  41.2 7.5 %all-to-all-done = bf16[32,2,3584]{2,1,0:T(2,128)(2,1)S(1)} async-done(((bf16[32,2,3584]{2,1,0:T(2,128)(2,1)}), bf16[32,2,3584]{2,1,0:T(2,128)(2,1)S(1)}, u32[]{:S(2)}, u32[]{:S(2)}) %all-to-all-start) | async-done | bytes 458784 | tf_op jit(solution)/shard_map/all_to_all | solution.py:45
  48.7 4.4 all-to-all-start.5
  53.5 2.6 bitcast_reduce_fusion
  57.7 5.0 all-to-all-done.5
  62.7 4.3 all-to-all-start.4
  67.0 2.6 add_convert_fusion.1
  69.7 1.6 copy.89
  71.2 5.3 all-to-all-done.4
  76.5 4.1 all-to-all-start.1
  83.0 19.3 %all-to-all-done.1 = bf16[64,7,1024]{2,1,0:T(8,128)(2,1)S(1)} async-done(((bf16[64,7,1024]{2,1,0:T(8,128)(2,1)}), bf16[64,7,1024]{2,1,0:T(8,128)(2,1)S(1)}, u32[]{:S(2)}, u32[]{:S(2)}) %all-to-all-start.1) | async-done | bytes 917536 | tf_op jit(solution)/shard_map/all_to_all | solution.py:66
  102.2 5.0 all-to-all-start.2
  109.8 1.8 copy.104
  114.1 2.2 copy.109
  116.3 2.3 copy.90
  118.6 6.3 %all-to-all-done.2 = bf16[64,7,1024]{2,1,0:T(8,128)(2,1)} async-done(((bf16[64,7,1024]{2,1,0:T(8,128)(2,1)}), bf16[64,7,1024]{2,1,0:T(8,128)(2,1)}, u32[]{:S(2)}, u32[]{:S(2)}) %all-to-all-start.2) | async-done | bytes 917536 | tf_op jit(solution)/shard_map/all_to_all | solution.py:69
  124.9 2.3 copy.93
  127.1 1.8 fusion.30
  129.0 1.8 fusion.34
  130.8 2.0 multiply_subtract_fusion
  132.9 2.5 fusion.20
  135.4 2.9 fusion.55
  138.2 2.7 fusion.53
  140.9 2.7 convolution_add_fusion.2
  143.6 3.8 fusion.29
  147.4 1.9 copy.114
  149.3 4.2 all-to-all-start.7
  153.5 1.9 copy.112
  155.4 10.4 %all-to-all-done.7 = bf16[2,224,1024]{2,0,1:T(2,128)(2,1)S(1)} async-done(((bf16[2,224,1024]{2,0,1:T(2,128)(2,1)}), bf16[2,224,1024]{2,0,1:T(2,128)(2,1)S(1)}, u32[]{:S(2)}, u32[]{:S(2)}) %all-to-all-start.7) | async-done | bytes 917536 | tf_op jit(solution)/shard_map/all_to_all | solution.py:106
  165.8 6.0 all-to-all-start.6
  172.7 19.2 %all-to-all-done.6 = bf16[2,224,1024]{2,0,1:T(2,128)(2,1)S(1)} async-done(((bf16[2,224,1024]{2,0,1:T(2,128)(2,1)}), bf16[2,224,1024]{2,0,1:T(2,128)(2,1)S(1)}, u32[]{:S(2)}, u32[]{:S(2)}) %all-to-all-start.6) | async-done | bytes 917536 | tf_op jit(solution)/shard_map/all_to_all | solution.py:103
  195.3 5.5 all-to-all-start.8
  201.0 10.9 %all-to-all-done.8 = bf16[32,7,1024]{2,1,0:T(8,128)(2,1)S(1)} async-done(((bf16[32,7,1024]{2,1,0:T(8,128)(2,1)}), bf16[32,7,1024]{2,1,0:T(8,128)(2,1)S(1)}, u32[]{:S(2)}, u32[]{:S(2)}) %all-to-all-start.8) | async-done | bytes 458784 | tf_op jit(solution)/shard_map/all_to_all | solution.py:113
  212.0 7.3 %fusion.37 = f32[224,4096]{1,0:T(8,128)} fusion(bf16[1024,4096]{1,0:T(8,128)(2,1)} %param.20, f32[224,1024]{1,0:T(8,128)S(1)} %reshape.181, bf16[224,1024]{1,0:T(8,128)(2,1)S(1)} %copy-done.6), kind=kOutput, calls=%fused_computation.63 | convolution fusion | flops 1879736320 | bytes 13434880 | tf_op jit(solution)/shard_map/dot_general | solution.py:196
  219.3 9.2 %copy.126 = bf16[896,8,8,128]{3,2,1,0:T(8,128)(2,1)S(1)} copy(bf16[896,8,8,128]{3,1,2,0:T(8,128)(2,1)} %bitcast.171) | data formatting | bytes 29360128
  228.6 7.3 %copy.117 = bf16[32,224,8,128]{3,1,2,0:T(8,128)(2,1)} copy(bf16[32,224,8,128]{3,2,1,0:T(8,128)(2,1)S(1)} %bitcast.169) | data formatting | bytes 29360128 | tf_op jit(solution)/shard_map/while | solution.py:175
  235.9 97.1 %all-gather.5.cloned.1.call-done = bf16[7168,1024]{1,0:T(8,128)(2,1)} async-done(((bf16[224,1024]{1,0:T(8,128)(2,1)}), bf16[7168,1024]{1,0:T(8,128)(2,1)}) %all-gather.5.cloned.1.call-update) | async-done | bytes 14680080 | tf_op jit(solution)/shard_map/all_gather | solution.py:158
  333.0 9.1 %copy.127 = bf16[896,8,8,128]{3,2,1,0:T(8,128)(2,1)S(1)} copy(bf16[896,8,8,128]{3,1,2,0:T(8,128)(2,1)} %bitcast.172) | data formatting | bytes 29360128
  342.1 7.3 %copy.119 = bf16[32,224,8,128]{3,1,2,0:T(8,128)(2,1)} copy(bf16[32,224,8,128]{3,2,1,0:T(8,128)(2,1)S(1)} %bitcast.170) | data formatting | bytes 29360128 | tf_op jit(solution)/shard_map/while | solution.py:175
  349.5 92.0 %while.14 = (s32[]{:T(128)}, f32[8,224]{1,0:T(8,128)S(1)}, f32[8,224]{1,0:T(8,128)S(1)}, f32[8,224,128]{2,1,0:T(8,128)S(1)}, s32[32]{0:T(128)S(1)}, /*index=5*/s...) while((s32[]{:T(128)}, f32[8,224]{1,0:T(8,128)S(1)}, ...), condition=%wide.region_5.6_spmd, body=%wide.region_0.5_spmd.sunk | while | flops 210449120 | bytes 8349359 | solution.py:175
  352.2 4.2 conditional.2
  352.4 1.5 fusion
  354.3 2.1 convolution_add_fusion
  441.5 7.9 %fusion.19 = bf16[224,4096]{1,0:T(8,128)(2,1)} fusion(f32[224,4096]{1,0:T(8,128)} %fusion.37, bf16[1024,4096]{1,0:T(8,128)(2,1)} %param.21, f32[8,224,128]{2,1,0:T(8,128)S(1)} %get-tuple-element.145, f32[8,224]{1,0:T(8,128)S(1)} %get-tuple-element.146), kind=kOutput, calls=%fused_computation.26 | convolution fusion | flops 1881341952 | bytes 14818304 | tf_op jit(solution)/shard_map/dot_general | solution.py:197
  449.4 155.4 %reduce-scatter.2.cloned.1.call-done = bf16[56,4096]{1,0:T(8,128)(2,1)} async-done(((bf16[224,4096]{1,0:T(8,128)(2,1)}), bf16[56,4096]{1,0:T(8,128)(2,1)}) %reduce-scatter.2.cloned.1.call-update) | async-done | bytes 458768 | tf_op jit(solution)/shard_map/reduce_scatter | solution.py:194
  (204 shorter events, 67.8 us)
Async XLA Ops:
  6.5 194.3 %copy-start = (bf16[224,1024]{1,0:T(8,128)(2,1)S(1)}, bf16[224,1024]{1,0:T(8,128)(2,1)}, u32[]{:S(2)}) copy-start(bf16[224,1024]{1,0:T(8,128)(2,1)} %param.17) | copy-start | bytes 1376260
  6.5 212.8 %all-gather.3.cloned.1.call-start = ((), (), s32[]{:S(2)}) async-start(), calls=%async_computation.10 | async-start | bytes 15138816 | tf_op jit(solution)/shard_map/all_gather | solution.py:157
  7.3 325.7 %all-gather.5.cloned.1.call-start = ((), (), s32[]{:S(2)}) async-start(), calls=%async_computation.11 | async-start | bytes 15138816 | tf_op jit(solution)/shard_map/all_gather | solution.py:158
  11.1 20.2 %all-to-all-start.3 = ((bf16[32,2,224]{2,1,0:T(2,128)(2,1)}), bf16[32,2,224]{2,1,0:T(2,128)(2,1)S(1)}, u32[]{:S(2)}, u32[]{:S(2)}) async-start(bf16[32,2,224]{2,1,0:T(2,128)(2,1)} %reshape.188), calls=%async_computation.3 | async-start | bytes 65536 | tf_op jit(solution)/shard_map/all_to_all | solution.py:48
  31.3 17.5 %all-to-all-start = ((bf16[32,2,3584]{2,1,0:T(2,128)(2,1)}), bf16[32,2,3584]{2,1,0:T(2,128)(2,1)S(1)}, u32[]{:S(2)}, u32[]{:S(2)}) async-start(bf16[32,2,3584]{2,1,0:T(2,128)(2,1)} %reshape.194), calls=%async_computation | async-start | bytes 917504 | tf_op jit(solution)/shard_map/all_to_all | solution.py:45
  48.7 14.0 %all-to-all-start.5 = ((bf16[32,2,448]{2,1,0:T(2,128)(2,1)}), bf16[32,2,448]{2,1,0:T(2,128)(2,1)S(1)}, u32[]{:S(2)}, u32[]{:S(2)}) async-start(bf16[32,2,448]{2,1,0:T(2,128)(2,1)} %reshape.192), calls=%async_computation.5 | async-start | bytes 131072 | tf_op jit(solution)/shard_map/all_to_all | solution.py:75
  62.7 13.8 %all-to-all-start.4 = ((bf16[32,2,448]{2,1,0:T(2,128)(2,1)}), bf16[32,2,448]{2,1,0:T(2,128)(2,1)S(1)}, u32[]{:S(2)}, u32[]{:S(2)}) async-start(bf16[32,2,448]{2,1,0:T(2,128)(2,1)} %reshape.190), calls=%async_computation.4 | async-start | bytes 131072 | tf_op jit(solution)/shard_map/all_to_all | solution.py:72
  71.2 10.2 %copy-start.5 = (bf16[64,7,1024]{2,0,1:T(8,128)(2,1)S(1)}, bf16[64,7,1024]{2,0,1:T(8,128)(2,1)}, u32[]{:S(2)}) copy-start(bf16[64,7,1024]{2,0,1:T(8,128)(2,1)} %get-tuple-element.199) | copy-start | bytes 2752516
  76.5 25.7 %all-to-all-start.1 = ((bf16[64,7,1024]{2,1,0:T(8,128)(2,1)}), bf16[64,7,1024]{2,1,0:T(8,128)(2,1)S(1)}, u32[]{:S(2)}, u32[]{:S(2)}) async-start(bf16[64,7,1024]{2,1,0:T(8,128)(2,1)} %copy.89), calls=%async_computation.1 | async-start | bytes 2097152 | tf_op jit(solution)/shard_map/all_to_all | solution.py:66
  102.2 6.2 %copy-start.4 = (bf16[64,7,1024]{2,1,0:T(8,128)(2,1)}, bf16[64,7,1024]{2,1,0:T(8,128)(2,1)S(1)}, u32[]{:S(2)}) copy-start(bf16[64,7,1024]{2,1,0:T(8,128)(2,1)S(1)} %all-to-all-done.1) | copy-start | bytes 2752516
  102.2 22.6 %all-to-all-start.2 = ((bf16[64,7,1024]{2,1,0:T(8,128)(2,1)}), bf16[64,7,1024]{2,1,0:T(8,128)(2,1)}, u32[]{:S(2)}, u32[]{:S(2)}) async-start(bf16[64,7,1024]{2,1,0:T(8,128)(2,1)} %copy.92), calls=%async_computation.2 | async-start | bytes 2097152 | tf_op jit(solution)/shard_map/all_to_all | solution.py:69
  130.8 2.0 copy-start.2
  130.8 2.0 copy-start.3
  149.3 16.5 %all-to-all-start.7 = ((bf16[2,224,1024]{2,0,1:T(2,128)(2,1)}), bf16[2,224,1024]{2,0,1:T(2,128)(2,1)S(1)}, u32[]{:S(2)}, u32[]{:S(2)}) async-start(bf16[2,224,1024]{2,0,1:T(2,128)(2,1)} %copy.114), calls=%async_computation.7 | async-start | bytes 1835008 | tf_op jit(solution)/shard_map/all_to_all | solution.py:106
  165.8 26.2 %all-to-all-start.6 = ((bf16[2,224,1024]{2,0,1:T(2,128)(2,1)}), bf16[2,224,1024]{2,0,1:T(2,128)(2,1)S(1)}, u32[]{:S(2)}, u32[]{:S(2)}) async-start(bf16[2,224,1024]{2,0,1:T(2,128)(2,1)} %copy.112), calls=%async_computation.6 | async-start | bytes 1835008 | tf_op jit(solution)/shard_map/all_to_all | solution.py:103
  195.3 16.7 %copy-start.6 = (bf16[224,1024]{1,0:T(8,128)(2,1)S(1)}, bf16[224,1024]{1,0:T(8,128)(2,1)}, u32[]{:S(2)}) copy-start(bf16[224,1024]{1,0:T(8,128)(2,1)} %param.13) | copy-start | bytes 1376260
  195.3 16.6 %all-to-all-start.8 = ((bf16[32,7,1024]{2,1,0:T(8,128)(2,1)}), bf16[32,7,1024]{2,1,0:T(8,128)(2,1)S(1)}, u32[]{:S(2)}, u32[]{:S(2)}) async-start(bf16[32,7,1024]{2,1,0:T(8,128)(2,1)} %copy.116), calls=%async_computation.8 | async-start | bytes 1048576 | tf_op jit(solution)/shard_map/all_to_all | solution.py:113
  200.8 404.0 %reduce-scatter.2.cloned.1.call-start = ((), (), s32[]{:S(2)}) async-start(), calls=%async_computation.12 | async-start | bytes 2293760 | tf_op jit(solution)/shard_map/reduce_scatter | solution.py:194
  441.5 163.3 %copy-start.1 = (bf16[224,1024]{1,0:T(8,128)(2,1)S(1)}, bf16[224,1024]{1,0:T(8,128)(2,1)}, u32[]{:S(2)}) copy-start(bf16[224,1024]{1,0:T(8,128)(2,1)} %param.17) | copy-start | bytes 1376260
Sparse Core Ops, SparseCore 0:
  10.4 179.5 all-gather.2
  193.1 139.8 all-gather.4
  449.5 155.2 reduce-scatter.1
where the time goes:
time: 622 us; the launch traced here: 612 us
  waiting for transfers between devices  340 us (55%)
  local copies, waits for them, and re-layouts  104 us (17%)
  starting transfers between devices  51.9 us (8%)
  matrix products  49.7 us (8%)
  loops' own time  45.7 us (7%)
  between operations  13.9 us (2%)
  other arithmetic  6.44 us (1%)
    reduce_scatter x1, waiting for transfers between devices, local(): lax.psum_scatter((jnp.dot(mixed, w_conv_out, preferred_element_type=jnp.f...  155 us
    all_gather x1, waiting for transfers between devices, attention(): value_piece = lax.all_gather(v_attn, 'ctx', axis=0, tiled=True)  97.1 us
    another operation x1, loops' own time, attention(): lax.scan(one_block, initial, (keys_split, values_split, jnp.arange(count_...  45.1 us
    unnamed x25, local copies, waits for them, and re-layouts  23 us
    dynamic_slice x32, local copies, waits for them, and re-layouts, attention(): lax.scan(one_block, initial, (keys_split, values_split, jnp.arange(count_...  21.2 us
    slice x32, local copies, waits for them, and re-layouts, one_block(): entry[1][-1]  20.8 us
    all_to_all x1, waiting for transfers between devices, spectral_conv(): lax.all_to_all(source_re.astype(jnp.bfloat16), 'ctx', split_axis=0, conca...  19.3 us
    all_to_all x1, waiting for transfers between devices, spectral_conv(): lax.all_to_all(turned_re.astype(jnp.bfloat16), 'ctx', split_axis=1, conca...  19.2 us
  transfers between devices with their start and end apart: 12, of which 11 were waited for; matrix products, arithmetic and copies ran while one was open for 14% of the time, Pallas kernels for 0%

commit v1 on v0

--- a/solution.py
+++ b/solution.py
@@ -100,8 +100,14 @@
     turned_re = back_re * cos_out - back_im * sin_out
     turned_im = back_re * sin_out + back_im * cos_out
     turned_re, turned_im = (
-        lax.all_to_all(
-            turned_re.astype(jnp.bfloat16), "ctx", split_axis=1, concat_axis=0, tiled=True
+        jnp.concatenate(
+            lax.all_to_all(
+                jnp.stack(jnp.split(turned_re.astype(jnp.bfloat16), lax.axis_size("ctx"), axis=1)),
+                "ctx",
+                0,
+                0,
+            ),
+            axis=0,
         ).astype(turned_re.dtype),
         lax.all_to_all(
             turned_im.astype(jnp.bfloat16), "ctx", split_axis=1, concat_axis=0, tiled=True

time: 622 us -> 622 us (level)
    unnamed x25 -> x56, local copies, waits for them, and re-layouts: 23 us -> 23.4 us
  transfers between devices with their start and end apart: 12 -> 12, of which waited for: 11 -> 11; matrix products, arithmetic and copies ran while one was open for 14% -> 15% of each run, Pallas kernels for 0% -> 0%
where the time goes in v1:
time: 622 us; the launch traced here: 611 us
  waiting for transfers between devices  339 us (55%)
  local copies, waits for them, and re-layouts  105 us (17%)
  starting transfers between devices  51.9 us (8%)
  matrix products  49.7 us (8%)
  loops' own time  45.6 us (7%)
  between operations  14.1 us (2%)
  other arithmetic  6.44 us (1%)
    reduce_scatter x1, waiting for transfers between devices, local(): lax.psum_scatter((jnp.dot(mixed, w_conv_out, preferred_element_type=jnp.f...  155 us
    all_gather x1, waiting for transfers between devices, attention(): value_piece = lax.all_gather(v_attn, 'ctx', axis=0, tiled=True)  97.1 us
    another operation x1, loops' own time, attention(): lax.scan(one_block, initial, (keys_split, values_split, jnp.arange(count_...  45.1 us
    unnamed x56, local copies, waits for them, and re-layouts  23.4 us
    dynamic_slice x32, local copies, waits for them, and re-layouts, attention(): lax.scan(one_block, initial, (keys_split, values_split, jnp.arange(count_...  21.2 us
    slice x32, local copies, waits for them, and re-layouts, one_block(): entry[1][-1]  20.8 us
    all_to_all x1, waiting for transfers between devices, spectral_conv(): lax.all_to_all(source_re.astype(jnp.bfloat16), 'ctx', split_axis=0, conca...  19.3 us
    all_to_all x1, waiting for transfers between devices, spectral_conv(): lax.all_to_all(jnp.stack(jnp.split(turned_re.astype(jnp.bfloat16), lax.ax...  19.2 us
  transfers between devices with their start and end apart: 12, of which 11 were waited for; matrix products, arithmetic and copies ran while one was open for 15% of the time, Pallas kernels for 0%

profile of v1, /device:TPU:1, one launch (start us, length us, event | category | flops | bytes accessed | tf_op | source)
XLA Modules:
  0.0 611.2 jit_solution(16669863039959866312)
XLA Ops:
  11.1 11.3 %all-to-all-start.3 = ((bf16[32,2,224]{2,1,0:T(2,128)(2,1)}), bf16[32,2,224]{2,1,0:T(2,128)(2,1)S(1)}, u32[]{:S(2)}, u32[]{:S(2)}) async-start(bf16[32,2,224]{2,1,0:T(2,128)(2,1)} %reshape.192), calls=%async_computation.3 | async-start | bytes 65536 | tf_op jit(solution)/shard_map/all_to_all | solution.py:48
  24.6 3.3 reduce.5
  29.0 2.2 all-to-all-done.3
  31.3 7.0 %all-to-all-start = ((bf16[32,2,3584]{2,1,0:T(2,128)(2,1)}), bf16[32,2,3584]{2,1,0:T(2,128)(2,1)S(1)}, u32[]{:S(2)}, u32[]{:S(2)}) async-start(bf16[32,2,3584]{2,1,0:T(2,128)(2,1)} %reshape.198), calls=%async_computation | async-start | bytes 917504 | tf_op jit(solution)/shard_map/all_to_all | solution.py:45
  41.2 7.5 %all-to-all-done = bf16[32,2,3584]{2,1,0:T(2,128)(2,1)S(1)} async-done(((bf16[32,2,3584]{2,1,0:T(2,128)(2,1)}), bf16[32,2,3584]{2,1,0:T(2,128)(2,1)S(1)}, u32[]{:S(2)}, u32[]{:S(2)}) %all-to-all-start) | async-done | bytes 458784 | tf_op jit(solution)/shard_map/all_to_all | solution.py:45
  48.7 4.4 all-to-all-start.5
  53.5 2.6 bitcast_reduce_fusion
  57.7 5.0 all-to-all-done.5
  62.7 4.3 all-to-all-start.4
  67.0 2.6 add_convert_fusion.1
  69.7 1.6 copy.88
  71.2 5.3 all-to-all-done.4
  76.5 4.1 all-to-all-start.1
  83.0 19.3 %all-to-all-done.1 = bf16[64,7,1024]{2,1,0:T(8,128)(2,1)S(1)} async-done(((bf16[64,7,1024]{2,1,0:T(8,128)(2,1)}), bf16[64,7,1024]{2,1,0:T(8,128)(2,1)S(1)}, u32[]{:S(2)}, u32[]{:S(2)}) %all-to-all-start.1) | async-done | bytes 917536 | tf_op jit(solution)/shard_map/all_to_all | solution.py:66
  102.2 5.0 all-to-all-start.2
  109.8 1.8 copy.103
  114.1 2.2 copy.108
  116.3 2.3 copy.89
  118.6 6.3 %all-to-all-done.2 = bf16[64,7,1024]{2,1,0:T(8,128)(2,1)} async-done(((bf16[64,7,1024]{2,1,0:T(8,128)(2,1)}), bf16[64,7,1024]{2,1,0:T(8,128)(2,1)}, u32[]{:S(2)}, u32[]{:S(2)}) %all-to-all-start.2) | async-done | bytes 917536 | tf_op jit(solution)/shard_map/all_to_all | solution.py:69
  124.9 2.3 copy.92
  127.1 1.8 fusion.30
  129.0 1.8 fusion.34
  130.8 2.0 multiply_subtract_fusion
  132.9 2.5 fusion.20
  135.4 2.9 fusion.55
  138.2 2.7 fusion.53
  140.9 2.7 convolution_add_fusion.2
  143.6 3.8 fusion.29
  147.4 1.9 copy.113
  149.3 4.2 all-to-all-start.7
  154.1 2.0 copy.111
  156.2 9.6 %all-to-all-done.7 = bf16[2,224,1024]{2,0,1:T(2,128)(2,1)S(1)} async-done(((bf16[2,224,1024]{2,0,1:T(2,128)(2,1)}), bf16[2,224,1024]{2,0,1:T(2,128)(2,1)S(1)}, u32[]{:S(2)}, u32[]{:S(2)}) %all-to-all-start.7) | async-done | bytes 917536 | tf_op jit(solution)/shard_map/all_to_all | solution.py:112
  165.8 6.0 all-to-all-start.6
  172.7 19.2 %all-to-all-done.6 = bf16[32,2,7,1024]{3,1,2,0:T(2,128)(2,1)S(1)} async-done(((bf16[32,2,7,1024]{3,1,2,0:T(2,128)(2,1)}), bf16[32,2,7,1024]{3,1,2,0:T(2,128)(2,1)S(1)}, u32[]{:S(2)}, u32[]{:S(2)}) %all-to-all-start.6) | async-done | bytes 917536 | tf_op jit(solution)/shard_map/all_to_all | solution.py:104
  195.3 5.5 all-to-all-start.8
  201.0 10.9 %all-to-all-done.8 = bf16[32,7,1024]{2,1,0:T(8,128)(2,1)S(1)} async-done(((bf16[32,7,1024]{2,1,0:T(8,128)(2,1)}), bf16[32,7,1024]{2,1,0:T(8,128)(2,1)S(1)}, u32[]{:S(2)}, u32[]{:S(2)}) %all-to-all-start.8) | async-done | bytes 458784 | tf_op jit(solution)/shard_map/all_to_all | solution.py:119
  212.0 7.3 %fusion.37 = f32[224,4096]{1,0:T(8,128)} fusion(bf16[1024,4096]{1,0:T(8,128)(2,1)} %param.20, f32[224,1024]{1,0:T(8,128)S(1)} %reshape.185, bf16[224,1024]{1,0:T(8,128)(2,1)S(1)} %copy-done.6), kind=kOutput, calls=%fused_computation.63 | convolution fusion | flops 1879736320 | bytes 13434880 | tf_op jit(solution)/shard_map/dot_general | solution.py:202
  219.3 9.2 %copy.125 = bf16[896,8,8,128]{3,2,1,0:T(8,128)(2,1)S(1)} copy(bf16[896,8,8,128]{3,1,2,0:T(8,128)(2,1)} %bitcast.296) | data formatting | bytes 29360128
  228.6 7.3 %copy.116 = bf16[32,224,8,128]{3,1,2,0:T(8,128)(2,1)} copy(bf16[32,224,8,128]{3,2,1,0:T(8,128)(2,1)S(1)} %bitcast.294) | data formatting | bytes 29360128 | tf_op jit(solution)/shard_map/while | solution.py:181
  235.9 97.1 %all-gather.5.cloned.1.call-done = bf16[7168,1024]{1,0:T(8,128)(2,1)} async-done(((bf16[224,1024]{1,0:T(8,128)(2,1)}), bf16[7168,1024]{1,0:T(8,128)(2,1)}) %all-gather.5.cloned.1.call-update) | async-done | bytes 14680080 | tf_op jit(solution)/shard_map/all_gather | solution.py:164
  333.0 9.1 %copy.126 = bf16[896,8,8,128]{3,2,1,0:T(8,128)(2,1)S(1)} copy(bf16[896,8,8,128]{3,1,2,0:T(8,128)(2,1)} %bitcast.297) | data formatting | bytes 29360128
  342.1 7.3 %copy.118 = bf16[32,224,8,128]{3,1,2,0:T(8,128)(2,1)} copy(bf16[32,224,8,128]{3,2,1,0:T(8,128)(2,1)S(1)} %bitcast.295) | data formatting | bytes 29360128 | tf_op jit(solution)/shard_map/while | solution.py:181
  349.5 91.9 %while.14 = (s32[]{:T(128)}, f32[8,224]{1,0:T(8,128)S(1)}, f32[8,224]{1,0:T(8,128)S(1)}, f32[8,224,128]{2,1,0:T(8,128)S(1)}, s32[32]{0:T(128)S(1)}, /*index=5*/s...) while((s32[]{:T(128)}, f32[8,224]{1,0:T(8,128)S(1)}, ...), condition=%wide.region_5.6_spmd, body=%wide.region_0.5_spmd.sunk | while | flops 210449120 | bytes 8349359 | solution.py:181
  352.2 4.2 conditional.2
  352.4 1.5 fusion
  354.3 2.1 convolution_add_fusion
  441.4 7.9 %fusion.19 = bf16[224,4096]{1,0:T(8,128)(2,1)} fusion(f32[224,4096]{1,0:T(8,128)} %fusion.37, bf16[1024,4096]{1,0:T(8,128)(2,1)} %param.21, f32[8,224,128]{2,1,0:T(8,128)S(1)} %get-tuple-element.145, f32[8,224]{1,0:T(8,128)S(1)} %get-tuple-element.146), kind=kOutput, calls=%fused_computation.26 | convolution fusion | flops 1881341952 | bytes 14818304 | tf_op jit(solution)/shard_map/dot_general | solution.py:203
  449.3 155.1 %reduce-scatter.2.cloned.1.call-done = bf16[56,4096]{1,0:T(8,128)(2,1)} async-done(((bf16[224,4096]{1,0:T(8,128)(2,1)}), bf16[56,4096]{1,0:T(8,128)(2,1)}) %reduce-scatter.2.cloned.1.call-update) | async-done | bytes 458768 | tf_op jit(solution)/shard_map/reduce_scatter | solution.py:200
  (236 shorter events, 68.1 us)
Async XLA Ops:
  6.5 194.3 %copy-start = (bf16[224,1024]{1,0:T(8,128)(2,1)S(1)}, bf16[224,1024]{1,0:T(8,128)(2,1)}, u32[]{:S(2)}) copy-start(bf16[224,1024]{1,0:T(8,128)(2,1)} %param.17) | copy-start | bytes 1376260
  6.5 212.8 %all-gather.3.cloned.1.call-start = ((), (), s32[]{:S(2)}) async-start(), calls=%async_computation.10 | async-start | bytes 15138816 | tf_op jit(solution)/shard_map/all_gather | solution.py:163
  7.3 325.7 %all-gather.5.cloned.1.call-start = ((), (), s32[]{:S(2)}) async-start(), calls=%async_computation.11 | async-start | bytes 15138816 | tf_op jit(solution)/shard_map/all_gather | solution.py:164
  11.1 20.2 %all-to-all-start.3 = ((bf16[32,2,224]{2,1,0:T(2,128)(2,1)}), bf16[32,2,224]{2,1,0:T(2,128)(2,1)S(1)}, u32[]{:S(2)}, u32[]{:S(2)}) async-start(bf16[32,2,224]{2,1,0:T(2,128)(2,1)} %reshape.192), calls=%async_computation.3 | async-start | bytes 65536 | tf_op jit(solution)/shard_map/all_to_all | solution.py:48
  31.3 17.5 %all-to-all-start = ((bf16[32,2,3584]{2,1,0:T(2,128)(2,1)}), bf16[32,2,3584]{2,1,0:T(2,128)(2,1)S(1)}, u32[]{:S(2)}, u32[]{:S(2)}) async-start(bf16[32,2,3584]{2,1,0:T(2,128)(2,1)} %reshape.198), calls=%async_computation | async-start | bytes 917504 | tf_op jit(solution)/shard_map/all_to_all | solution.py:45
  48.7 14.0 %all-to-all-start.5 = ((bf16[32,2,448]{2,1,0:T(2,128)(2,1)}), bf16[32,2,448]{2,1,0:T(2,128)(2,1)S(1)}, u32[]{:S(2)}, u32[]{:S(2)}) async-start(bf16[32,2,448]{2,1,0:T(2,128)(2,1)} %reshape.196), calls=%async_computation.5 | async-start | bytes 131072 | tf_op jit(solution)/shard_map/all_to_all | solution.py:75
  62.7 13.8 %all-to-all-start.4 = ((bf16[32,2,448]{2,1,0:T(2,128)(2,1)}), bf16[32,2,448]{2,1,0:T(2,128)(2,1)S(1)}, u32[]{:S(2)}, u32[]{:S(2)}) async-start(bf16[32,2,448]{2,1,0:T(2,128)(2,1)} %reshape.194), calls=%async_computation.4 | async-start | bytes 131072 | tf_op jit(solution)/shard_map/all_to_all | solution.py:72
  71.2 10.2 %copy-start.5 = (bf16[64,7,1024]{2,0,1:T(8,128)(2,1)S(1)}, bf16[64,7,1024]{2,0,1:T(8,128)(2,1)}, u32[]{:S(2)}) copy-start(bf16[64,7,1024]{2,0,1:T(8,128)(2,1)} %get-tuple-element.199) | copy-start | bytes 2752516
  76.5 25.7 %all-to-all-start.1 = ((bf16[64,7,1024]{2,1,0:T(8,128)(2,1)}), bf16[64,7,1024]{2,1,0:T(8,128)(2,1)S(1)}, u32[]{:S(2)}, u32[]{:S(2)}) async-start(bf16[64,7,1024]{2,1,0:T(8,128)(2,1)} %copy.88), calls=%async_computation.1 | async-start | bytes 2097152 | tf_op jit(solution)/shard_map/all_to_all | solution.py:66
  102.2 6.2 %copy-start.4 = (bf16[64,7,1024]{2,1,0:T(8,128)(2,1)}, bf16[64,7,1024]{2,1,0:T(8,128)(2,1)S(1)}, u32[]{:S(2)}) copy-start(bf16[64,7,1024]{2,1,0:T(8,128)(2,1)S(1)} %all-to-all-done.1) | copy-start | bytes 2752516
  102.2 22.6 %all-to-all-start.2 = ((bf16[64,7,1024]{2,1,0:T(8,128)(2,1)}), bf16[64,7,1024]{2,1,0:T(8,128)(2,1)}, u32[]{:S(2)}, u32[]{:S(2)}) async-start(bf16[64,7,1024]{2,1,0:T(8,128)(2,1)} %copy.91), calls=%async_computation.2 | async-start | bytes 2097152 | tf_op jit(solution)/shard_map/all_to_all | solution.py:69
  130.8 2.0 copy-start.2
  130.8 2.0 copy-start.3
  149.3 16.5 %all-to-all-start.7 = ((bf16[2,224,1024]{2,0,1:T(2,128)(2,1)}), bf16[2,224,1024]{2,0,1:T(2,128)(2,1)S(1)}, u32[]{:S(2)}, u32[]{:S(2)}) async-start(bf16[2,224,1024]{2,0,1:T(2,128)(2,1)} %copy.113), calls=%async_computation.7 | async-start | bytes 1835008 | tf_op jit(solution)/shard_map/all_to_all | solution.py:112
  165.8 26.2 %all-to-all-start.6 = ((bf16[32,2,7,1024]{3,1,2,0:T(2,128)(2,1)}), bf16[32,2,7,1024]{3,1,2,0:T(2,128)(2,1)S(1)}, u32[]{:S(2)}, u32[]{:S(2)}) async-start(bf16[32,2,7,1024]{3,1,2,0:T(2,128)(2,1)} %copy.111), calls=%async_computation.6 | async-start | bytes 1835008 | tf_op jit(solution)/shard_map/all_to_all | solution.py:104
  195.3 16.7 %copy-start.6 = (bf16[224,1024]{1,0:T(8,128)(2,1)S(1)}, bf16[224,1024]{1,0:T(8,128)(2,1)}, u32[]{:S(2)}) copy-start(bf16[224,1024]{1,0:T(8,128)(2,1)} %param.13) | copy-start | bytes 1376260
  195.3 16.6 %all-to-all-start.8 = ((bf16[32,7,1024]{2,1,0:T(8,128)(2,1)}), bf16[32,7,1024]{2,1,0:T(8,128)(2,1)S(1)}, u32[]{:S(2)}, u32[]{:S(2)}) async-start(bf16[32,7,1024]{2,1,0:T(8,128)(2,1)} %copy.115), calls=%async_computation.8 | async-start | bytes 1048576 | tf_op jit(solution)/shard_map/all_to_all | solution.py:119
  200.8 403.7 %reduce-scatter.2.cloned.1.call-start = ((), (), s32[]{:S(2)}) async-start(), calls=%async_computation.12 | async-start | bytes 2293760 | tf_op jit(solution)/shard_map/reduce_scatter | solution.py:200
  441.4 163.0 %copy-start.1 = (bf16[224,1024]{1,0:T(8,128)(2,1)S(1)}, bf16[224,1024]{1,0:T(8,128)(2,1)}, u32[]{:S(2)}) copy-start(bf16[224,1024]{1,0:T(8,128)(2,1)} %param.17) | copy-start | bytes 1376260
Sparse Core Ops, SparseCore 0:
  10.4 179.5 all-gather.2
  193.1 139.8 all-gather.4
  449.4 154.9 reduce-scatter.1
